TPU v7x, 32 devices: a whole 2x2x4 slice. The times are simulated.
32 devices in a mesh: uv: 8 (over z, y), rep: 4 (over x, core).
Axes of the slice: x: 2, y: 2, z: 4, core: 2. Of those that a mesh axis runs over, the one named last changes fastest.
Arguments:
- visibilities: float32 [2, 32, 8, 16, 12], P(None, ('uv', 'rep')), may hold values from -6 to 6
- tile_counts: int32 [32, 8, 16], P(('uv', 'rep')), may hold values from 2 to 12, as said below
- w_plane: int32 [32, 8, 16, 12], P(('uv', 'rep')), may hold values from 0 to 63
- u_offset: int32 [32, 8, 16, 12], P(('uv', 'rep')), may hold values from 0 to 120
- v_offset: int32 [32, 8, 16, 12], P(('uv', 'rep')), may hold values from 0 to 120
- kernels: float32 [64, 128], replicated, may hold values from -2.5 to 2.5
Outputs:
- spectrum: float32 [2048, 2, 1024], P(('uv', 'rep'))
Inputs may be any that keep to these rules, and one draw needn't show every extreme that they name: `tile_counts`: every source device's list for tile 16//2 of destination column 4 holds 12 visibilities; tiles near the grid's centre are fuller than others.
All inputs are finite; a program needn't handle non-finite values.
Results may differ from a plain program's by a relative error of at most 0.0029.
Values may be sent and summed in bfloat16 or wider, within the bound.
No kernel may reach another device: no remote copies, remote signals or barrier semaphores. Data moves between devices by JAX's collectives and lax.ppermute only.
A program may use at most 192 MiB of HBM per device.

v0:
```python
import math
import jax
import jax.numpy as jnp
from jax import lax
from jax.sharding import PartitionSpec as P

TILE = 128
SUPPORT = 8


def weigh(vis_re, vis_im, planes, kernels):
    nplanes = kernels.shape[0]
    width = kernels.shape[1]
    half = width // 2
    onehot = (
        planes[..., None] == lax.broadcasted_iota(jnp.int32, planes.shape + (nplanes,), planes.ndim)
    ).astype(jnp.float32)
    kern = jnp.dot(
        onehot.reshape(-1, nplanes),
        kernels,
        precision=lax.Precision.HIGHEST,
        preferred_element_type=jnp.float32,
    )
    kern = kern.reshape(planes.shape + (width,))
    kern_re = kern[..., :half]
    kern_im = kern[..., half:]
    part_re = vis_re[..., None] * kern_re - vis_im[..., None] * kern_im
    part_im = vis_re[..., None] * kern_im + vis_im[..., None] * kern_re
    return jnp.concatenate([part_re, part_im], axis=-1).astype(jnp.bfloat16)


def grid_tiles(weighted, row_start, col_start):
    senders = weighted.shape[0]
    ntiles = weighted.shape[1]
    slots = weighted.shape[2]
    count = senders * slots
    per_tile = jnp.moveaxis(weighted, 1, 0).reshape(ntiles, count, 2, SUPPORT, SUPPORT)
    rows_all = jnp.moveaxis(row_start, 1, 0).reshape(ntiles, count)
    cols_all = jnp.moveaxis(col_start, 1, 0).reshape(ntiles, count)
    lanes = lax.broadcasted_iota(jnp.int32, (1, SUPPORT, TILE), 2)
    taps = lax.broadcasted_iota(jnp.int32, (1, SUPPORT, TILE), 1)
    cells = lax.broadcasted_iota(jnp.int32, (TILE, 1, SUPPORT), 0)
    taps_row = lax.broadcasted_iota(jnp.int32, (TILE, 1, SUPPORT), 2)

    def one_tile(operands):
        values, row_first, col_first = operands
        place = (lanes == col_first[:, None, None] + taps).astype(jnp.bfloat16)
        spread = jnp.einsum("ncij,njb->nicb", values, place)
        spread = spread.reshape(count * SUPPORT, 2 * TILE)
        pick = (cells == row_first[None, :, None] + taps_row).astype(jnp.bfloat16)
        pick = pick.reshape(TILE, count * SUPPORT)
        summed = jnp.dot(pick, spread, preferred_element_type=jnp.float32)
        return summed.reshape(TILE, 2, TILE)

    return lax.map(one_tile, (per_tile, rows_all, cols_all))


def make_table(first, second, length):
    index_a = lax.broadcasted_iota(jnp.int32, (first, second), 0)
    index_b = lax.broadcasted_iota(jnp.int32, (first, second), 1)
    angle = 2.0 * math.pi / length * (index_a * index_b % length).astype(jnp.float32)
    return (jnp.cos(angle), jnp.sin(angle))


def transform(pencil):
    nrows = pencil.shape[0]
    groups = lax.axis_size("uv")
    total = pencil.shape[2]
    width = total // groups
    highest = lax.Precision.HIGHEST
    cos_a, sin_a = make_table(groups, groups, groups)
    cos_t, sin_t = make_table(groups, width, total)
    cos_b, sin_b = make_table(width, width, width)
    field = pencil.reshape(nrows, 2, groups, width)
    real_in = field[:, 0]
    imag_in = field[:, 1]
    first_re = jnp.einsum("rpj,pk->rkj", real_in, cos_a, precision=highest) + jnp.einsum(
        "rpj,pk->rkj", imag_in, sin_a, precision=highest
    )
    first_im = jnp.einsum("rpj,pk->rkj", imag_in, cos_a, precision=highest) - jnp.einsum(
        "rpj,pk->rkj", real_in, sin_a, precision=highest
    )
    turned_re = first_re * cos_t + first_im * sin_t
    turned_im = first_im * cos_t - first_re * sin_t
    final_re = jnp.einsum("rkj,jm->rmk", turned_re, cos_b, precision=highest) + jnp.einsum(
        "rkj,jm->rmk", turned_im, sin_b, precision=highest
    )
    final_im = jnp.einsum("rkj,jm->rmk", turned_im, cos_b, precision=highest) - jnp.einsum(
        "rkj,jm->rmk", turned_re, sin_b, precision=highest
    )
    scale = 1.0 / math.sqrt(total)
    return (
        jnp.stack([final_re.reshape(nrows, total), final_im.reshape(nrows, total)], axis=1) * scale
    )


def shards(visibilities, tile_counts, w_plane, u_offset, v_offset, kernels):
    dests = visibilities.shape[2]
    ntiles = visibilities.shape[3]
    slots = visibilities.shape[4]
    nuv = lax.axis_size("uv")
    nrep = lax.axis_size("rep")
    per_device = ntiles * TILE // (nuv * nrep)
    live = (
        lax.broadcasted_iota(jnp.int32, (dests, ntiles, slots), 2) < tile_counts[0][:, :, None]
    ).astype(jnp.float32)
    vis_re = visibilities[0, 0] * live
    vis_im = visibilities[1, 0] * live
    weighted = weigh(vis_re, vis_im, w_plane[0], kernels)
    slab = grid_tiles(
        lax.all_to_all(weighted, "uv", split_axis=0, concat_axis=0, tiled=True),
        lax.all_to_all(u_offset[0], "uv", split_axis=0, concat_axis=0, tiled=True),
        lax.all_to_all(v_offset[0], "uv", split_axis=0, concat_axis=0, tiled=True),
    )
    blocks = slab.reshape(nuv, nrep, per_device, 2, TILE)
    moved_rows = lax.all_to_all(blocks, "uv", split_axis=0, concat_axis=4, tiled=True)
    pencil = lax.psum_scatter(moved_rows, "rep", scatter_dimension=1, tiled=True)
    pencil = pencil.reshape(per_device, 2, nuv * TILE)
    return transform(pencil)


def solution(mesh):
    placed = (
        P(None, ("uv", "rep"), None, None, None),
        P(("uv", "rep"), None, None),
        P(("uv", "rep"), None, None, None),
        P(("uv", "rep"), None, None, None),
        P(("uv", "rep"), None, None, None),
        P(),
    )
    return jax.shard_map(
        shards, mesh=mesh, in_specs=placed, out_specs=P(("uv", "rep"), None, None), check_vma=False
    )
```

profile of v0, /device:TPU:0, one launch (start us, length us, event | category | flops | bytes accessed | tf_op | source)
XLA Modules:
  0.0 184.7 jit_solution(3883717939173195149)
XLA Ops:
  8.1 7.3 %all-to-all-start = ((s32[8,1,192]{2,1,0:T(1,128)}), s32[8,1,192]{2,1,0:T(1,128)S(1)}, u32[]{:S(2)}, u32[]{:S(2)}) async-start(s32[8,1,192]{2,1,0:T(1,128)} %reshape.171), calls=%async_computation | async-start | bytes 16384 | tf_op jit(solution)/shard_map/all_to_all | solution.py:112
  19.3 2.6 %all-to-all-done = s32[8,1,192]{2,1,0:T(1,128)S(1)} async-done(((s32[8,1,192]{2,1,0:T(1,128)}), s32[8,1,192]{2,1,0:T(1,128)S(1)}, u32[]{:S(2)}, u32[]{:S(2)}) %all-to-all-start) | async-done | bytes 6176 | tf_op jit(solution)/shard_map/all_to_all | solution.py:112
  21.8 3.4 %all-to-all-start.1 = ((s32[8,1,192]{2,1,0:T(1,128)}), s32[8,1,192]{2,1,0:T(1,128)S(1)}, u32[]{:S(2)}, u32[]{:S(2)}) async-start(s32[8,1,192]{2,1,0:T(1,128)} %reshape.173), calls=%async_computation.1 | async-start | bytes 16384 | tf_op jit(solution)/shard_map/all_to_all | solution.py:113
  26.2 5.5 %all-to-all-done.1 = s32[8,1,192]{2,1,0:T(1,128)S(1)} async-done(((s32[8,1,192]{2,1,0:T(1,128)}), s32[8,1,192]{2,1,0:T(1,128)S(1)}, u32[]{:S(2)}, u32[]{:S(2)}) %all-to-all-start.1) | async-done | bytes 6176 | tf_op jit(solution)/shard_map/all_to_all | solution.py:113
  31.8 3.5 %all-to-all-start.2 = ((bf16[8,16,12,128]{3,1,2,0:T(8,128)(2,1)}), bf16[8,16,12,128]{3,1,2,0:T(8,128)(2,1)S(1)}, u32[]{:S(2)}, u32[]{:S(2)}) async-start(bf16[8,16,12,128]{3,1,2,0:T(8,128)(2,1)} %pad_maximum_fusion), calls=%async_computation.2 | async-start | bytes 786432 | tf_op jit(solution)/shard_map/all_to_all | solution.py:111
  37.6 7.5 %all-to-all-done.2 = bf16[8,16,12,128]{3,1,2,0:T(8,128)(2,1)S(1)} async-done(((bf16[8,16,12,128]{3,1,2,0:T(8,128)(2,1)}), bf16[8,16,12,128]{3,1,2,0:T(8,128)(2,1)S(1)}, u32[]{:S(2)}, u32[]{:S(2)}) %all-to-all-start.2) | async-done | bytes 393248 | tf_op jit(solution)/shard_map/all_to_all | solution.py:111
  45.3 8.5 %reshape.170 = bf16[16,96,2,8,8]{4,3,2,1,0:T(8,128)(2,1)} reshape(bf16[16,8,12,128]{3,2,1,0:T(8,128)(2,1)S(1)} %copy.99) | data formatting | bytes 786432
  53.7 31.8 %while.13 = (s32[]{:T(128)}, f32[16,128,2,128]{3,1,0,2:T(8,128)S(1)}, s32[16,96]{1,0:T(8,128)S(1)}, s32[16,96]{1,0:T(8,128)S(1)}, bf16[16,96,2,8,8]{4,3,2,1,0:T(8,128)(2,1)}, /*index=5*/s32[]{:T(128)}) while((s32[]{:T(128)}, f32[16,128,2,128]{3,1,0,2:T(8,128)S(1)}, s32[16,96]{1,0:T(8,128)S(1)}, s32[16,96]{1,0:T(8,128)S(1)}, ...), condition=%wide.region_1.2_spmd.clone.clone, body=%wide.region_0.1_spmd.clone.clone.sunk | while | flops 53773056 | bytes 2113357 | solution.py:55
  55.7 1.3 convolution_bitcast_fusion.3
  57.7 1.3 convolution_bitcast_fusion.3
  59.7 1.3 convolution_bitcast_fusion.3
  61.7 1.3 convolution_bitcast_fusion.3
  63.7 1.3 convolution_bitcast_fusion.3
  65.7 1.3 convolution_bitcast_fusion.3
  67.7 1.3 convolution_bitcast_fusion.3
  69.6 1.3 convolution_bitcast_fusion.3
  71.6 1.3 convolution_bitcast_fusion.3
  73.6 1.3 convolution_bitcast_fusion.3
  75.6 1.3 convolution_bitcast_fusion.3
  77.6 1.3 convolution_bitcast_fusion.3
  81.6 1.3 convolution_bitcast_fusion.3
  85.8 50.9 %all_to_all.33 = f32[8,4,64,2,128]{4,2,1,3,0:T(8,128)S(1)} all-to-all(f32[8,4,64,2,128]{4,2,1,3,0:T(8,128)S(1)} %copy.83), channel_id=1, replica_groups=mesh['uv'=8,'rep'=4] {'uv'}, dimensions={0} | all-to-all | bytes 4194304 | tf_op jit(solution)/shard_map/all_to_all | solution.py:116
  137.9 2.0 %copy.85 = f32[1,4,64,2,1024]{4,2,3,0,1:T(8,128)} copy(f32[1,4,64,2,1024]{4,0,3,2,1:T(1,128)S(1)} %bitcast.143) | data formatting | bytes 4194304 | tf_op jit(solution)/shard_map/all_to_all | solution.py:116
  139.9 30.4 %reduce-scatter.2.cloned.1.call-done = f32[1,1,64,2,1024]{4,2,3,0,1:T(8,128)} async-done(((f32[1,4,64,2,1024]{4,2,3,0,1:T(8,128)}), f32[1,1,64,2,1024]{4,2,3,0,1:T(8,128)}) %reduce-scatter.2.cloned.1.call-update) | async-done | bytes 524304 | tf_op jit(solution)/shard_map/reduce_scatter | solution.py:117
  (131 shorter events, 31.8 us)
Async XLA Ops:
  6.5 10.5 %copy-start = (f32[64,128]{1,0:T(8,128)S(1)}, f32[64,128]{1,0:T(8,128)}, u32[]{:S(2)}) copy-start(f32[64,128]{1,0:T(8,128)} %param.13) | copy-start | bytes 98308
  6.5 12.0 %copy-start.1 = (s32[1,8,16,12]{2,1,3,0:T(8,128)S(1)}, s32[1,8,16,12]{2,1,3,0:T(8,128)}, u32[]{:S(2)}) copy-start(s32[1,8,16,12]{2,1,3,0:T(8,128)} %param.12) | copy-start | bytes 18436
  8.1 13.8 %all-to-all-start = ((s32[8,1,192]{2,1,0:T(1,128)}), s32[8,1,192]{2,1,0:T(1,128)S(1)}, u32[]{:S(2)}, u32[]{:S(2)}) async-start(s32[8,1,192]{2,1,0:T(1,128)} %reshape.171), calls=%async_computation | async-start | bytes 16384 | tf_op jit(solution)/shard_map/all_to_all | solution.py:112
  21.8 9.9 %all-to-all-start.1 = ((s32[8,1,192]{2,1,0:T(1,128)}), s32[8,1,192]{2,1,0:T(1,128)S(1)}, u32[]{:S(2)}, u32[]{:S(2)}) async-start(s32[8,1,192]{2,1,0:T(1,128)} %reshape.173), calls=%async_computation.1 | async-start | bytes 16384 | tf_op jit(solution)/shard_map/all_to_all | solution.py:113
  31.8 13.4 %all-to-all-start.2 = ((bf16[8,16,12,128]{3,1,2,0:T(8,128)(2,1)}), bf16[8,16,12,128]{3,1,2,0:T(8,128)(2,1)S(1)}, u32[]{:S(2)}, u32[]{:S(2)}) async-start(bf16[8,16,12,128]{3,1,2,0:T(8,128)(2,1)} %pad_maximum_fusion), calls=%async_computation.2 | async-start | bytes 786432 | tf_op jit(solution)/shard_map/all_to_all | solution.py:111
  35.2 135.1 %reduce-scatter.2.cloned.1.call-start = ((), (), s32[]{:S(2)}) async-start(), calls=%async_computation.5 | async-start | bytes 2621440 | tf_op jit(solution)/shard_map/reduce_scatter | solution.py:117
Sparse Core Ops, SparseCore 0:
  140.0 30.3 reduce-scatter.1
where the time goes:
time: 186 us; the launch traced here: 185 us
  blocking collectives  50.9 us (27%)
  waiting for transfers between devices  46.1 us (25%)
  matrix products  30.6 us (16%)
  local copies, waits for them, and re-layouts  23.5 us (13%)
  starting transfers between devices  14.2 us (8%)
  between operations  13.7 us (7%)
  other arithmetic  5.16 us (3%)
    all_to_all x1, blocking collectives, shards(): lax.all_to_all(blocks, 'uv', split_axis=0, concat_axis=4, tiled=True)  50.9 us
    reduce_scatter x1, waiting for transfers between devices, shards(): lax.psum_scatter(moved_rows, 'rep', scatter_dimension=1, tiled=True)  30.4 us
    dot_general x16, matrix products, one_tile(): spread = jnp.einsum('ncij,njb->nicb', values, place)  20.9 us
    unnamed x13, local copies, waits for them, and re-layouts  12.1 us
    all_to_all x1, waiting for transfers between devices, shards(): lax.all_to_all(weighted, 'uv', split_axis=0, concat_axis=0, tiled=True)  7.5 us
    all_to_all x1, starting transfers between devices, shards(): lax.all_to_all(u_offset[0], 'uv', split_axis=0, concat_axis=0, tiled=True)  7.28 us
    all_to_all x1, waiting for transfers between devices, shards(): lax.all_to_all(v_offset[0], 'uv', split_axis=0, concat_axis=0, tiled=True)  5.54 us
    dot_general x16, matrix products, one_tile(): summed = jnp.dot(pick, spread, preferred_element_type=jnp.float32)  4.67 us
  transfers between devices with their start and end apart: 4, of which 4 were waited for; matrix products, arithmetic and copies ran while one was open for 4% of the time, Pallas kernels for 0%

commit v1 on v0

--- a/solution.py
+++ b/solution.py
@@ -6,6 +6,20 @@
 
 TILE = 128
 SUPPORT = 8
+
+
+def update_samples_all(view, which_dim, vector):
+    prior, state_next = (view.shape[:which_dim], view.shape[which_dim + 1 :])
+    arr_out = view.reshape(*prior, vector, -1, *state_next)
+    return jnp.moveaxis(arr_out, which_dim, 0)
+
+
+def raise_the_strings(frame_in, axis_k):
+    frame_in = jnp.moveaxis(frame_in, 0, axis_k)
+    w_next = frame_in.shape
+    return frame_in.reshape(
+        *w_next[:axis_k], w_next[axis_k] * w_next[axis_k + 1], *w_next[axis_k + 2 :]
+    )
 
 
 def weigh(vis_re, vis_im, planes, kernels):
@@ -107,9 +121,26 @@
     vis_re = visibilities[0, 0] * live
     vis_im = visibilities[1, 0] * live
     weighted = weigh(vis_re, vis_im, w_plane[0], kernels)
+
+    def columns_keep_up(local_values, mesh_ax, obj, a0):
+        q_next = lax.axis_size(mesh_ax)
+        known = lax.axis_index(mesh_ax)
+        h_now, answer = (q_next, known)
+        tall = update_samples_all(local_values, obj, h_now)
+        arrivals = [tall[answer]]
+        idx = 1
+        while idx < h_now:
+            f_next = tall[(answer + idx) % h_now]
+            r_now = lax.ppermute(f_next, mesh_ax, [(j, (j + idx) % h_now) for j in range(h_now)])
+            arrivals.append(r_now)
+            idx = idx + 1
+        then = jnp.stack(arrivals, axis=0)
+        tall = then[(answer - jnp.arange(h_now)) % h_now]
+        return raise_the_strings(tall, a0)
+
     slab = grid_tiles(
         lax.all_to_all(weighted, "uv", split_axis=0, concat_axis=0, tiled=True),
-        lax.all_to_all(u_offset[0], "uv", split_axis=0, concat_axis=0, tiled=True),
+        columns_keep_up(u_offset[0], "uv", 0, 0),
         lax.all_to_all(v_offset[0], "uv", split_axis=0, concat_axis=0, tiled=True),
     )
     blocks = slab.reshape(nuv, nrep, per_device, 2, TILE)

time: 186 us -> 184 us (0.989)
  waiting for transfers between devices: 46.1 us -> 34.8 us
  starting transfers between devices: 14.2 us -> 25.2 us
    ppermute x0 -> x7, starting transfers between devices: none -> 14.2 us  [columns_keep_up(): lax.ppermute(f_next, mesh_ax, [(j, (j + idx) % h_now) for j in range(h_no...]
    all_to_all x1, waiting for transfers between devices: 7.5 us -> 0.01 us  [shards(): lax.all_to_all(weighted, 'uv', split_axis=0, concat_axis=0, tiled=True)]
    all_to_all x1 -> x0, starting transfers between devices: 7.28 us -> none  [shards(): lax.all_to_all(u_offset[0], 'uv', split_axis=0, concat_axis=0, tiled=True)]
    all_to_all x1, starting transfers between devices: 3.42 us -> 7.28 us  [shards(): lax.all_to_all(v_offset[0], 'uv', split_axis=0, concat_axis=0, tiled=True)]
    all_to_all x1, waiting for transfers between devices: 5.54 us -> 2.33 us  [shards(): lax.all_to_all(v_offset[0], 'uv', split_axis=0, concat_axis=0, tiled=True)]
    all_to_all x1 -> x0, waiting for transfers between devices: 2.59 us -> none  [shards(): lax.all_to_all(u_offset[0], 'uv', split_axis=0, concat_axis=0, tiled=True)]
    ppermute x0 -> x7, waiting for transfers between devices: none -> 1.92 us  [columns_keep_up(): lax.ppermute(f_next, mesh_ax, [(j, (j + idx) % h_now) for j in range(h_no...]
    unnamed x13 -> x10, local copies, waits for them, and re-layouts: 12.1 us -> 11.4 us
  transfers between devices with their start and end apart: 4 -> 10, of which waited for: 4 -> 3; matrix products, arithmetic and copies ran while one was open for 4% -> 3% of each run, Pallas kernels for 0% -> 0%
where the time goes in v1:
time: 184 us; the launch traced here: 182 us
  blocking collectives  49.6 us (27%)
  waiting for transfers between devices  34.8 us (19%)
  matrix products  30.6 us (17%)
  starting transfers between devices  25.2 us (14%)
  local copies, waits for them, and re-layouts  23.5 us (13%)
  between operations  13.8 us (8%)
  other arithmetic  4.33 us (2%)
    all_to_all x1, blocking collectives, shards(): lax.all_to_all(blocks, 'uv', split_axis=0, concat_axis=4, tiled=True)  49.6 us
    reduce_scatter x1, waiting for transfers between devices, shards(): lax.psum_scatter(moved_rows, 'rep', scatter_dimension=1, tiled=True)  30.5 us
    dot_general x16, matrix products, one_tile(): spread = jnp.einsum('ncij,njb->nicb', values, place)  20.9 us
    ppermute x7, starting transfers between devices, columns_keep_up(): lax.ppermute(f_next, mesh_ax, [(j, (j + idx) % h_now) for j in range(h_no...  14.2 us
    unnamed x10, local copies, waits for them, and re-layouts  11.4 us
    all_to_all x1, starting transfers between devices, shards(): lax.all_to_all(v_offset[0], 'uv', split_axis=0, concat_axis=0, tiled=True)  7.28 us
    dot_general x16, matrix products, one_tile(): summed = jnp.dot(pick, spread, preferred_element_type=jnp.float32)  4.67 us
  transfers between devices with their start and end apart: 10, of which 3 were waited for; matrix products, arithmetic and copies ran while one was open for 3% of the time, Pallas kernels for 0%

profile of v1, /device:TPU:0, one launch (start us, length us, event | category | flops | bytes accessed | tf_op | source)
XLA Modules:
  0.0 182.4 jit_solution(13228872202872873279)
XLA Ops:
  8.1 7.3 %all-to-all-start = ((s32[8,1,192]{2,1,0:T(1,128)}), s32[8,1,192]{2,1,0:T(1,128)S(1)}, u32[]{:S(2)}, u32[]{:S(2)}) async-start(s32[8,1,192]{2,1,0:T(1,128)} %reshape.249), calls=%async_computation | async-start | bytes 16384 | tf_op jit(solution)/shard_map/all_to_all | solution.py:144
  19.5 2.3 %all-to-all-done = s32[8,1,192]{2,1,0:T(1,128)S(1)} async-done(((s32[8,1,192]{2,1,0:T(1,128)}), s32[8,1,192]{2,1,0:T(1,128)S(1)}, u32[]{:S(2)}, u32[]{:S(2)}) %all-to-all-start) | async-done | bytes 6176 | tf_op jit(solution)/shard_map/all_to_all | solution.py:144
  21.9 3.7 %all-to-all-start.1 = ((bf16[8,16,12,128]{3,1,2,0:T(8,128)(2,1)}), bf16[8,16,12,128]{3,1,2,0:T(8,128)(2,1)S(1)}, u32[]{:S(2)}, u32[]{:S(2)}) async-start(bf16[8,16,12,128]{3,1,2,0:T(8,128)(2,1)} %pad_maximum_fusion), calls=%async_computation.1 | async-start | bytes 786432 | tf_op jit(solution)/shard_map/all_to_all | solution.py:142
  25.7 3.7 %collective-permute-start.4 = (s32[1,16,12]{1,0,2:T(1,128)S(1)}, s32[1,16,12]{1,0,2:T(1,128)S(1)}, u32[]{:S(2)}, u32[]{:S(2)}) collective-permute-start(s32[1,16,12]{1,0,2:T(1,128)S(1)} %get-tuple-element.152), channel_id=1, source_target_pairs={{0,20},{4,24},{8,28},{12,0},{16,4},{20,8},{24,12},{28,16},{1,21},{... | collective-permute-start | bytes 2312 | tf_op jit(solution)/shard_map/ppermute | solution.py:134
  29.5 1.5 collective-permute-start.5
  31.5 1.5 collective-permute-start
  33.5 3.8 %collective-permute-start.2 = (s32[1,16,12]{1,0,2:T(1,128)S(1)}, s32[1,16,12]{1,0,2:T(1,128)S(1)}, u32[]{:S(2)}, u32[]{:S(2)}) collective-permute-start(s32[1,16,12]{1,0,2:T(1,128)S(1)} %get-tuple-element.154), channel_id=1, source_target_pairs={{0,12},{4,16},{8,20},{12,24},{16,28},{20,0},{24,4},{28,8},{1,13},{... | collective-permute-start | bytes 2312 | tf_op jit(solution)/shard_map/ppermute | solution.py:134
  37.3 2.6 %collective-permute-start.3 = (s32[1,16,12]{1,0,2:T(1,128)S(1)}, s32[1,16,12]{1,0,2:T(1,128)S(1)}, u32[]{:S(2)}, u32[]{:S(2)}) collective-permute-start(s32[1,16,12]{1,0,2:T(1,128)S(1)} %get-tuple-element.153), channel_id=1, source_target_pairs={{0,16},{4,20},{8,24},{12,28},{16,0},{20,4},{24,8},{28,12},{1,17},{... | collective-permute-start | bytes 2312 | tf_op jit(solution)/shard_map/ppermute | solution.py:134
  40.0 1.9 %collective-permute-done.3 = s32[1,16,12]{1,0,2:T(1,128)S(1)} collective-permute-done((s32[1,16,12]{1,0,2:T(1,128)S(1)}, s32[1,16,12]{1,0,2:T(1,128)S(1)}, u32[]{:S(2)}, u32[]{:S(2)}) %collective-permute-start.3) | collective-permute-done | bytes 800 | tf_op jit(solution)/shard_map/ppermute | solution.py:134
  44.1 8.5 %reshape.248 = bf16[16,96,2,8,8]{4,3,2,1,0:T(8,128)(2,1)} reshape(bf16[16,8,12,128]{3,2,1,0:T(8,128)(2,1)S(1)} %copy.103) | data formatting | bytes 786432
  52.6 31.8 %while.13 = (s32[]{:T(128)}, f32[16,128,2,128]{3,1,0,2:T(8,128)S(1)}, s32[16,96]{1,0:T(8,128)S(1)}, s32[16,96]{1,0:T(8,128)S(1)}, bf16[16,96,2,8,8]{4,3,2,1,0:T(8,128)(2,1)}, /*index=5*/s32[]{:T(128)}) while((s32[]{:T(128)}, f32[16,128,2,128]{3,1,0,2:T(8,128)S(1)}, s32[16,96]{1,0:T(8,128)S(1)}, s32[16,96]{1,0:T(8,128)S(1)}, ...), condition=%wide.region_1.2_spmd.clone.clone, body=%wide.region_0.1_spmd.clone.clone.sunk | while | flops 53773056 | bytes 2113357 | solution.py:69
  54.6 1.3 convolution_bitcast_fusion.3
  56.6 1.3 convolution_bitcast_fusion.3
  58.6 1.3 convolution_bitcast_fusion.3
  60.6 1.3 convolution_bitcast_fusion.3
  62.6 1.3 convolution_bitcast_fusion.3
  64.6 1.3 convolution_bitcast_fusion.3
  66.5 1.3 convolution_bitcast_fusion.3
  68.5 1.3 convolution_bitcast_fusion.3
  70.5 1.3 convolution_bitcast_fusion.3
  74.5 1.3 convolution_bitcast_fusion.3
  84.7 49.6 %all_to_all.28 = f32[8,4,64,2,128]{4,2,1,3,0:T(8,128)S(1)} all-to-all(f32[8,4,64,2,128]{4,2,1,3,0:T(8,128)S(1)} %copy.88), channel_id=1, replica_groups=mesh['uv'=8,'rep'=4] {'uv'}, dimensions={0} | all-to-all | bytes 4194304 | tf_op jit(solution)/shard_map/all_to_all | solution.py:147
  135.5 2.0 %copy.90 = f32[1,4,64,2,1024]{4,2,3,0,1:T(8,128)} copy(f32[1,4,64,2,1024]{4,0,3,2,1:T(1,128)S(1)} %bitcast.156) | data formatting | bytes 4194304 | tf_op jit(solution)/shard_map/all_to_all | solution.py:147
  137.6 30.5 %reduce-scatter.2.cloned.1.call-done = f32[1,1,64,2,1024]{4,2,3,0,1:T(8,128)} async-done(((f32[1,4,64,2,1024]{4,2,3,0,1:T(8,128)}), f32[1,1,64,2,1024]{4,2,3,0,1:T(8,128)}) %reduce-scatter.2.cloned.1.call-update) | async-done | bytes 524304 | tf_op jit(solution)/shard_map/reduce_scatter | solution.py:148
  (144 shorter events, 36.0 us)
Async XLA Ops:
  6.5 10.5 %copy-start = (f32[64,128]{1,0:T(8,128)S(1)}, f32[64,128]{1,0:T(8,128)}, u32[]{:S(2)}) copy-start(f32[64,128]{1,0:T(8,128)} %param.13) | copy-start | bytes 98308
  8.1 13.8 %all-to-all-start = ((s32[8,1,192]{2,1,0:T(1,128)}), s32[8,1,192]{2,1,0:T(1,128)S(1)}, u32[]{:S(2)}, u32[]{:S(2)}) async-start(s32[8,1,192]{2,1,0:T(1,128)} %reshape.249), calls=%async_computation | async-start | bytes 16384 | tf_op jit(solution)/shard_map/all_to_all | solution.py:144
  17.9 7.8 %copy-start.1 = (s32[1,8,16,12]{2,1,3,0:T(8,128)S(1)}, s32[1,8,16,12]{2,1,3,0:T(8,128)}, u32[]{:S(2)}) copy-start(s32[1,8,16,12]{2,1,3,0:T(8,128)} %param.11) | copy-start | bytes 18436
  21.9 22.1 %all-to-all-start.1 = ((bf16[8,16,12,128]{3,1,2,0:T(8,128)(2,1)}), bf16[8,16,12,128]{3,1,2,0:T(8,128)(2,1)S(1)}, u32[]{:S(2)}, u32[]{:S(2)}) async-start(bf16[8,16,12,128]{3,1,2,0:T(8,128)(2,1)} %pad_maximum_fusion), calls=%async_computation.1 | async-start | bytes 786432 | tf_op jit(solution)/shard_map/all_to_all | solution.py:142
  25.5 142.6 %reduce-scatter.2.cloned.1.call-start = ((), (), s32[]{:S(2)}) async-start(), calls=%async_computation.4 | async-start | bytes 2621440 | tf_op jit(solution)/shard_map/reduce_scatter | solution.py:148
  25.7 7.8 %collective-permute-start.4 = (s32[1,16,12]{1,0,2:T(1,128)S(1)}, s32[1,16,12]{1,0,2:T(1,128)S(1)}, u32[]{:S(2)}, u32[]{:S(2)}) collective-permute-start(s32[1,16,12]{1,0,2:T(1,128)S(1)} %get-tuple-element.152), channel_id=1, source_target_pairs={{0,20},{4,24},{8,28},{12,0},{16,4},{20,8},{24,12},{28,16},{1,21},{... | collective-permute-start | bytes 2312 | tf_op jit(solution)/shard_map/ppermute | solution.py:134
  29.5 7.9 %collective-permute-start.5 = (s32[1,16,12]{1,0,2:T(1,128)S(1)}, s32[1,16,12]{1,0,2:T(1,128)S(1)}, u32[]{:S(2)}, u32[]{:S(2)}) collective-permute-start(s32[1,16,12]{1,0,2:T(1,128)S(1)} %get-tuple-element.158), channel_id=1, source_target_pairs={{0,24},{4,28},{8,0},{12,4},{16,8},{20,12},{24,16},{28,20},{1,25},{... | collective-permute-start | bytes 2312 | tf_op jit(solution)/shard_map/ppermute | solution.py:134
  30.9 9.0 %collective-permute-start.6 = (s32[1,16,12]{1,0,2:T(1,128)S(1)}, s32[1,16,12]{1,0,2:T(1,128)S(1)}, u32[]{:S(2)}, u32[]{:S(2)}) collective-permute-start(s32[1,16,12]{1,0,2:T(1,128)S(1)} %get-tuple-element.151), channel_id=1, source_target_pairs={{0,28},{4,0},{8,4},{12,8},{16,12},{20,16},{24,20},{28,24},{1,29},{... | collective-permute-start | bytes 2312 | tf_op jit(solution)/shard_map/ppermute | solution.py:134
  31.5 8.5 %collective-permute-start = (s32[1,16,12]{1,0,2:T(1,128)S(1)}, s32[1,16,12]{1,0,2:T(1,128)S(1)}, u32[]{:S(2)}, u32[]{:S(2)}) collective-permute-start(s32[1,16,12]{1,0,2:T(1,128)S(1)} %get-tuple-element.156), channel_id=1, source_target_pairs={{0,4},{4,8},{8,12},{12,16},{16,20},{20,24},{24,28},{28,0},{1,5},{5... | collective-permute-start | bytes 2312 | tf_op jit(solution)/shard_map/ppermute | solution.py:134
  33.0 7.0 %collective-permute-start.1 = (s32[1,16,12]{1,0,2:T(1,128)S(1)}, s32[1,16,12]{1,0,2:T(1,128)S(1)}, u32[]{:S(2)}, u32[]{:S(2)}) collective-permute-start(s32[1,16,12]{1,0,2:T(1,128)S(1)} %get-tuple-element.155), channel_id=1, source_target_pairs={{0,8},{4,12},{8,16},{12,20},{16,24},{20,28},{24,0},{28,4},{1,9},{5... | collective-permute-start | bytes 2312 | tf_op jit(solution)/shard_map/ppermute | solution.py:134
  33.5 6.4 %collective-permute-start.2 = (s32[1,16,12]{1,0,2:T(1,128)S(1)}, s32[1,16,12]{1,0,2:T(1,128)S(1)}, u32[]{:S(2)}, u32[]{:S(2)}) collective-permute-start(s32[1,16,12]{1,0,2:T(1,128)S(1)} %get-tuple-element.154), channel_id=1, source_target_pairs={{0,12},{4,16},{8,20},{12,24},{16,28},{20,0},{24,4},{28,8},{1,13},{... | collective-permute-start | bytes 2312 | tf_op jit(solution)/shard_map/ppermute | solution.py:134
  37.3 4.5 %collective-permute-start.3 = (s32[1,16,12]{1,0,2:T(1,128)S(1)}, s32[1,16,12]{1,0,2:T(1,128)S(1)}, u32[]{:S(2)}, u32[]{:S(2)}) collective-permute-start(s32[1,16,12]{1,0,2:T(1,128)S(1)} %get-tuple-element.153), channel_id=1, source_target_pairs={{0,16},{4,20},{8,24},{12,28},{16,0},{20,4},{24,8},{28,12},{1,17},{... | collective-permute-start | bytes 2312 | tf_op jit(solution)/shard_map/ppermute | solution.py:134
Sparse Core Ops, SparseCore 0:
  137.6 30.4 reduce-scatter.1
